TPU v7x, 256 devices: a whole 4x4x8 slice. The times are simulated.
256 devices in a mesh: seq: 64 (over y, z, core), head: 4 (over x).
Axes of the slice: x: 4, y: 4, z: 8, core: 2. Of those that a mesh axis runs over, the one named last changes fastest.
Arguments:
- queries: bfloat16 [32768, 4096], P(('seq', 'head')), may hold values from -6 to 6
- keys: bfloat16 [32768, 4096], P(('seq', 'head')), may hold values from -6 to 6
- values: bfloat16 [32768, 4096], P(('seq', 'head')), may hold values from -6 to 6
- cluster_ids: int32 [32, 32768, 1], P(None, 'seq'), may hold values from 0 to 127; in each aligned block of 128 rows (0 to 127, 128 to 255, ..., all dimensions but the last counted through in order) at most 2 rows name the same one
- out_weight: bfloat16 [4096, 4096], P('head', 'seq'), may hold values from -0.09375 to 0.09375
Outputs:
- projected: bfloat16 [32768, 4096], P('seq', 'head')
Inputs may be any that keep to these rules, and one draw needn't show every extreme that they name: `cluster_ids`: in each aligned block of 128 tokens of one head (the rows of one device), no cluster id appears more than 2 times, and some cluster appears exactly 2 times.
All inputs are finite; a program needn't handle non-finite values.
Results may differ from a plain program's by a relative error of at most 0.014.
Values may be sent and summed in bfloat16 or wider, within the bound.
No kernel may reach another device: no remote copies, remote signals or barrier semaphores. Data moves between devices by JAX's collectives and lax.ppermute only.
A program may use at most 128 MiB of HBM per device.

v0:
```python
import jax
import jax.numpy as jnp
from jax import lax
from jax.sharding import PartitionSpec as P

HEADS = 32
HD = 128
CLUSTERS = 128


def slot_table(block_ids, slot_depth):
    sub_rows = block_ids.shape[-1]
    onehot = (block_ids[..., None] == jnp.arange(CLUSTERS, dtype=jnp.int32)).astype(jnp.float32)
    lower = (jnp.arange(sub_rows)[:, None] >= jnp.arange(sub_rows)[None, :]).astype(jnp.float32)
    running = jnp.einsum("ts,abse->abte", lower, onehot)
    ranking = (jnp.sum(running * onehot, axis=-1) - 1.0).astype(jnp.int32)
    depth_hit = (ranking[..., None] == jnp.arange(slot_depth, dtype=jnp.int32)).astype(jnp.bfloat16)
    return onehot.astype(jnp.bfloat16)[..., :, None] * depth_hit[..., None, :]


def attend_blocks(packed, validity):
    scores = jnp.einsum(
        "cqd,ckd->cqk", packed[0], packed[1], preferred_element_type=jnp.float32
    ) * HD ** (-0.5)
    scores = jnp.where(validity[:, None, :] > 0, scores, -1e30)
    row_max = jnp.max(scores, axis=-1, keepdims=True)
    raised = jnp.exp(scores - row_max)
    weights = (raised / jnp.sum(raised, axis=-1, keepdims=True)).astype(jnp.bfloat16)
    return jnp.einsum(
        "cqk,ckd->cqd", weights, packed[2], preferred_element_type=jnp.float32
    ).astype(jnp.bfloat16)


def attend_and_return(arrived):
    packed, markers = arrived
    item_count = packed.shape[1]
    n_seq = packed.shape[2]
    lane_count = packed.shape[3]
    result_block = attend_blocks(
        packed.reshape(3, item_count, n_seq * lane_count, HD),
        markers.reshape(item_count, n_seq * lane_count),
    )
    result_block = result_block.reshape(item_count, n_seq, lane_count, HD)
    return lax.all_to_all(result_block, "seq", split_axis=1, concat_axis=1, tiled=True)


def body(queries, keys, values, cluster_ids, out_weight):
    n_seq = lax.axis_size("seq")
    n_head = lax.axis_size("head")
    head_group = lax.axis_index("head")
    tok_dev = cluster_ids.shape[1]
    sub_rows = tok_dev // n_head
    group_heads = HEADS // n_head
    slot_depth = max(2, 2 * tok_dev // (n_head * CLUSTERS))
    lane_count = n_head * slot_depth
    per_owner = group_heads * CLUSTERS // n_seq
    all_ids = cluster_ids[:, :, 0]
    group_ids = lax.dynamic_slice_in_dim(all_ids, head_group * group_heads, group_heads, 0)
    group_ids = group_ids.reshape(group_heads, n_head, sub_rows)
    home_table = slot_table(group_ids, slot_depth)
    relaid = (
        lax.all_to_all(queries, "head", split_axis=1, concat_axis=0, tiled=True),
        lax.all_to_all(keys, "head", split_axis=1, concat_axis=0, tiled=True),
        lax.all_to_all(values, "head", split_axis=1, concat_axis=0, tiled=True),
    )
    stacked = jnp.stack([tensor.reshape(n_head, sub_rows, group_heads, HD) for tensor in relaid])
    packed = jnp.einsum(
        "hltcr,xlthd->xhclrd", home_table, stacked, preferred_element_type=jnp.float32
    ).astype(jnp.bfloat16)
    packed = packed.reshape(3, per_owner, n_seq, lane_count, HD)
    markers = (
        jnp.sum(home_table.astype(jnp.float32), axis=2).transpose(0, 2, 1, 3).astype(jnp.bfloat16)
    )
    markers = markers.reshape(1, per_owner, n_seq, lane_count)
    returned = attend_and_return(
        (
            lax.all_to_all(packed, "seq", split_axis=2, concat_axis=2, tiled=True),
            lax.all_to_all(markers, "seq", split_axis=2, concat_axis=2, tiled=True),
        )
    )
    returned = returned.reshape(group_heads, CLUSTERS, n_head, slot_depth, HD)
    gathered = jnp.einsum(
        "hltcr,hclrd->lthd", home_table, returned, preferred_element_type=jnp.float32
    ).astype(jnp.bfloat16)
    gathered = gathered.reshape(tok_dev, group_heads * HD)
    partial_value = jnp.dot(
        gathered,
        lax.all_gather(out_weight, "seq", axis=1, tiled=True),
        preferred_element_type=jnp.float32,
    )
    return lax.psum_scatter(
        partial_value.astype(jnp.bfloat16), "head", scatter_dimension=1, tiled=True
    )


def solution(mesh):
    in_specs = (
        P(("seq", "head"), None),
        P(("seq", "head"), None),
        P(("seq", "head"), None),
        P(None, "seq", None),
        P("head", "seq"),
    )
    out_specs = P("seq", "head")
    return jax.shard_map(body, mesh=mesh, in_specs=in_specs, out_specs=out_specs, check_vma=False)
```

profile of v0, /device:TPU:1, one launch (start us, length us, event | category | flops | bytes accessed | tf_op | source)
XLA Modules:
  0.0 417.8 jit_solution(13506348038587240276)
XLA Ops:
  6.5 2.4 copy.54
  8.9 4.8 %all-to-all-start.1 = ((bf16[128,4,1024]{0,2,1:T(8,128)(2,1)}), bf16[128,4,1024]{0,2,1:T(8,128)(2,1)S(1)}, u32[]{:S(2)}, u32[]{:S(2)}) async-start(bf16[128,4,1024]{0,2,1:T(8,128)(2,1)} %bitcast.6), calls=%async_computation.1 | async-start | bytes 2097152 | tf_op jit(solution)/shard_map/all_to_all | solution.py:62
  13.7 1.3 copy.55
  15.1 11.9 %all-to-all-done.1 = bf16[128,4,1024]{0,2,1:T(8,128)(2,1)S(1)} async-done(((bf16[128,4,1024]{0,2,1:T(8,128)(2,1)}), bf16[128,4,1024]{0,2,1:T(8,128)(2,1)S(1)}, u32[]{:S(2)}, u32[]{:S(2)}) %all-to-all-start.1) | async-done | bytes 1048608 | tf_op jit(solution)/shard_map/all_to_all | solution.py:62
  27.0 3.5 all-to-all-start.2
  30.5 2.3 copy.56
  32.8 1.2 convert_convert_fusion
  34.0 8.5 %all-to-all-done.2 = bf16[128,4,1024]{0,2,1:T(8,128)(2,1)S(1)} async-done(((bf16[128,4,1024]{0,2,1:T(8,128)(2,1)}), bf16[128,4,1024]{0,2,1:T(8,128)(2,1)S(1)}, u32[]{:S(2)}, u32[]{:S(2)}) %all-to-all-start.2) | async-done | bytes 1048608 | tf_op jit(solution)/shard_map/all_to_all | solution.py:63
  42.5 4.2 %all-to-all-start.3 = ((bf16[128,4,1024]{0,2,1:T(8,128)(2,1)}), bf16[128,4,1024]{0,2,1:T(8,128)(2,1)}, u32[]{:S(2)}, u32[]{:S(2)}) async-start(bf16[128,4,1024]{0,2,1:T(8,128)(2,1)} %bitcast.12), calls=%async_computation.3 | async-start | bytes 2097152 | tf_op jit(solution)/shard_map/all_to_all | solution.py:64
  47.4 1.6 copy.49
  49.1 2.5 multiply_reduce_fusion
  51.7 0.8 copy.52
  52.5 1.3 copy.57
  53.8 1.3 copy.58
  55.1 2.5 all-to-all-done.3
  57.6 19.1 %all-to-all-start = ((bf16[1,16,64,8]{1,3,0,2:T(8,128)(2,1)}), bf16[1,16,64,8]{1,3,0,2:T(8,128)(2,1)S(1)}, u32[]{:S(2)}, u32[]{:S(2)}) async-start(bf16[1,16,64,8]{1,3,0,2:T(8,128)(2,1)} %copy.52), calls=%async_computation | async-start | bytes 262144 | tf_op jit(solution)/shard_map/all_to_all | solution.py:78
  76.7 1.6 copy.59
  78.4 3.8 convert_bitcast_fusion
  82.1 2.6 copy.61
  84.8 6.7 %copy.62 = bf16[3,16,64,8,128]{4,1,3,0,2:T(8,128)(2,1)} copy(bf16[3,16,64,8,128]{4,2,1,3,0:T(8,128)(2,1)S(1)} %bitcast.66) | data formatting | bytes 12582912 | tf_op jit(solution)/shard_map/reshape | solution.py:70
  91.4 10.5 %all-to-all-start.4 = ((bf16[3,16,64,8,128]{4,1,3,0,2:T(8,128)(2,1)}), bf16[3,16,64,8,128]{4,1,3,0,2:T(8,128)(2,1)}, u32[]{:S(2)}, u32[]{:S(2)}) async-start(bf16[3,16,64,8,128]{4,1,3,0,2:T(8,128)(2,1)} %copy.62), calls=%async_computation.4 | async-start | bytes 12582912 | tf_op jit(solution)/shard_map/all_to_all | solution.py:77
  103.1 164.3 %all-to-all-done.4 = bf16[3,16,64,8,128]{4,1,3,0,2:T(8,128)(2,1)} async-done(((bf16[3,16,64,8,128]{4,1,3,0,2:T(8,128)(2,1)}), bf16[3,16,64,8,128]{4,1,3,0,2:T(8,128)(2,1)}, u32[]{:S(2)}, u32[]{:S(2)}) %all-to-all-start.4) | async-done | bytes 6291488 | tf_op jit(solution)/shard_map/all_to_all | solution.py:77
  267.4 6.0 %fusion.45 = (bf16[1,16,64,8,128]{4,1,3,0,2:T(8,128)(2,1)S(1)}, bf16[1,16,64,8,128]{4,1,3,0,2:T(8,128)(2,1)}, bf16[1,16,64,8,128]{4,1,3,0,2:T(8,128)(2,1)S(1)}) fusion(bf16[3,16,64,8,128]{4,1,3,0,2:T(8,128)(2,1)} %all-to-all-done.4), kind=kLoop, calls=%fused_computation.52 | loop fusion | bytes 12582912 | tf_op jit(solution)/shard_map/slice | solution.py:23
  273.4 2.4 fusion.14
  275.8 8.1 %fusion.46 = (f32[16,512]{1,0:T(8,128)S(1)}, f32[16,512,512]{1,2,0:T(8,128)}) fusion(f32[16,512,512]{1,2,0:T(8,128)S(1)} %fusion.14, pred[16,512]{1,0:T(8,128)(4,1)S(1)} %copy.53), kind=kOutput, calls=%fused_computation.53 | output fusion | flops 25166336 | bytes 33595392 | tf_op jit(solution)/shard_map/sub | solution.py:27
  283.9 9.4 %convert_bitcast_fusion.1 = bf16[16,64,8,128]{3,2,1,0:T(8,128)(2,1)S(1)} fusion(bf16[1,16,64,8,128]{4,1,3,0,2:T(8,128)(2,1)} %get-tuple-element.6, f32[16,512,512]{1,2,0:T(8,128)} %get-tuple-element.11, f32[16,512]{1,0:T(8,128)S(1)} %get-tuple-element.10), kind=kOutput, calls=%fused_computation.32 | convolution fusion | flops 1083179008 | bytes 21004288 | tf_op jit(solution)/shard_map/cqk,ckd->cqd/dot_general | solution.py:29
  293.3 2.4 copy.67
  295.8 56.8 %all_to_all.63 = bf16[16,64,8,128]{3,0,2,1:T(8,128)(2,1)S(1)} all-to-all(bf16[16,64,8,128]{3,0,2,1:T(8,128)(2,1)S(1)} %copy.67), channel_id=1, replica_groups=mesh['seq'=64,'head'=4] {'seq'}, dimensions={1} | all-to-all | bytes 4194304 | tf_op jit(solution)/shard_map/all_to_all | solution.py:44
  352.6 1.4 copy.68
  354.0 2.6 fusion.29
  357.3 9.5 %convolution_convert_fusion = bf16[512,4096]{1,0:T(8,128)(2,1)} fusion(bf16[1024,4096]{0,1:T(8,128)(2,1)} %all-gather.2.cloned.1.call-done, bf16[64,8,8,128]{3,2,1,0:T(8,128)(2,1)S(1)} %bitcast.70), kind=kOutput, calls=%fused_computation.10 | convolution fusion | flops 4297064448 | bytes 13631488 | tf_op jit(solution)/shard_map/dot_general | solution.py:86
  366.8 44.2 %reduce-scatter.2.cloned.1.call-done = bf16[512,1024]{1,0:T(8,128)(2,1)} async-done(((bf16[512,4096]{1,0:T(8,128)(2,1)}), bf16[512,1024]{1,0:T(8,128)(2,1)}) %reduce-scatter.2.cloned.1.call-update) | async-done | bytes 1048592 | tf_op jit(solution)/shard_map/reduce_scatter | solution.py:91
  (23 shorter events, 2.7 us)
Async XLA Ops:
  6.5 26.2 %copy-start = (s32[32,512,1]{1,2,0:T(1,128)S(1)}, s32[32,512,1]{1,2,0:T(1,128)}, u32[]{:S(2)}) copy-start(s32[32,512,1]{1,2,0:T(1,128)} %param.8) | copy-start | bytes 196612
  6.5 7.2 %copy-start.2 = (bf16[128,4096]{1,0:T(8,128)(2,1)S(1)}, bf16[128,4096]{1,0:T(8,128)(2,1)}, u32[]{:S(2)}) copy-start(bf16[128,4096]{1,0:T(8,128)(2,1)} %param.6) | copy-start | bytes 3145732
  8.9 18.1 %all-to-all-start.1 = ((bf16[128,4,1024]{0,2,1:T(8,128)(2,1)}), bf16[128,4,1024]{0,2,1:T(8,128)(2,1)S(1)}, u32[]{:S(2)}, u32[]{:S(2)}) async-start(bf16[128,4,1024]{0,2,1:T(8,128)(2,1)} %bitcast.6), calls=%async_computation.1 | async-start | bytes 2097152 | tf_op jit(solution)/shard_map/all_to_all | solution.py:62
  27.0 15.5 %all-to-all-start.2 = ((bf16[128,4,1024]{0,2,1:T(8,128)(2,1)}), bf16[128,4,1024]{0,2,1:T(8,128)(2,1)S(1)}, u32[]{:S(2)}, u32[]{:S(2)}) async-start(bf16[128,4,1024]{0,2,1:T(8,128)(2,1)} %bitcast.9), calls=%async_computation.2 | async-start | bytes 2097152 | tf_op jit(solution)/shard_map/all_to_all | solution.py:63
  42.5 15.1 %all-to-all-start.3 = ((bf16[128,4,1024]{0,2,1:T(8,128)(2,1)}), bf16[128,4,1024]{0,2,1:T(8,128)(2,1)}, u32[]{:S(2)}, u32[]{:S(2)}) async-start(bf16[128,4,1024]{0,2,1:T(8,128)(2,1)} %bitcast.12), calls=%async_computation.3 | async-start | bytes 2097152 | tf_op jit(solution)/shard_map/all_to_all | solution.py:64
  53.8 24.6 %copy-start.3 = (bf16[1,4,128,8,128]{4,2,0,1,3:T(8,128)(2,1)S(1)}, bf16[1,4,128,8,128]{4,2,0,1,3:T(8,128)(2,1)}, u32[]{:S(2)}) copy-start(bf16[1,4,128,8,128]{4,2,0,1,3:T(8,128)(2,1)} %copy.57) | copy-start | bytes 3145732
  57.6 33.8 %all-to-all-start = ((bf16[1,16,64,8]{1,3,0,2:T(8,128)(2,1)}), bf16[1,16,64,8]{1,3,0,2:T(8,128)(2,1)S(1)}, u32[]{:S(2)}, u32[]{:S(2)}) async-start(bf16[1,16,64,8]{1,3,0,2:T(8,128)(2,1)} %copy.52), calls=%async_computation | async-start | bytes 262144 | tf_op jit(solution)/shard_map/all_to_all | solution.py:78
  91.4 175.9 %all-to-all-start.4 = ((bf16[3,16,64,8,128]{4,1,3,0,2:T(8,128)(2,1)}), bf16[3,16,64,8,128]{4,1,3,0,2:T(8,128)(2,1)}, u32[]{:S(2)}, u32[]{:S(2)}) async-start(bf16[3,16,64,8,128]{4,1,3,0,2:T(8,128)(2,1)} %copy.62), calls=%async_computation.4 | async-start | bytes 12582912 | tf_op jit(solution)/shard_map/all_to_all | solution.py:77
  101.9 255.3 %all-gather.2.cloned.1.call-start = ((), (), s32[]{:S(2)}) async-start(), calls=%async_computation.7 | async-start | bytes 8519680 | tf_op jit(solution)/shard_map/all_gather | solution.py:88
  102.7 308.3 %reduce-scatter.2.cloned.1.call-start = ((), (), s32[]{:S(2)}) async-start(), calls=%async_computation.8 | async-start | bytes 5242880 | tf_op jit(solution)/shard_map/reduce_scatter | solution.py:91
  357.3 53.7 %copy-start.1 = (s32[32,512,1]{1,2,0:T(1,128)S(1)}, s32[32,512,1]{1,2,0:T(1,128)}, u32[]{:S(2)}) copy-start(s32[32,512,1]{1,2,0:T(1,128)} %param.8) | copy-start | bytes 196612
Sparse Core Ops, SparseCore 0:
  105.6 134.2 all-gather.1
  366.9 43.9 reduce-scatter.1
where the time goes:
time: 418 us
  waiting for transfers between devices  232 us (56%)
  blocking collectives  56.8 us (14%)
  starting transfers between devices  42.5 us (10%)
  local copies, waits for them, and re-layouts  32.7 us (8%)
  matrix products  28.3 us (7%)
  between operations  13.6 us (3%)
  other arithmetic  11.9 us (3%)
    all_to_all x1, waiting for transfers between devices, body(): lax.all_to_all(packed, 'seq', split_axis=2, concat_axis=2, tiled=True)  164 us
    all_to_all x1, blocking collectives, attend_and_return(): lax.all_to_all(result_block, 'seq', split_axis=1, concat_axis=1, tiled=True)  56.8 us
    reduce_scatter x1, waiting for transfers between devices, body(): lax.psum_scatter(partial_value.astype(jnp.bfloat16), 'head', scatter_dime...  44.2 us
    all_to_all x1, starting transfers between devices, body(): lax.all_to_all(markers, 'seq', split_axis=2, concat_axis=2, tiled=True)  19.1 us
    all_to_all x1, waiting for transfers between devices, body(): lax.all_to_all(queries, 'head', split_axis=1, concat_axis=0, tiled=True)  11.9 us
    all_to_all x1, starting transfers between devices, body(): lax.all_to_all(packed, 'seq', split_axis=2, concat_axis=2, tiled=True)  10.5 us
    dot_general x1, matrix products, body(): jnp.dot(gathered, lax.all_gather(out_weight, 'seq', axis=1, tiled=True),...  9.49 us
    dot_general x1, matrix products, attend_blocks(): jnp.einsum('cqk,ckd->cqd', weights, packed[2], preferred_element_type=jnp...  9.4 us
  transfers between devices with their start and end apart: 7, of which 5 were waited for; matrix products, arithmetic and copies ran while one was open for 15% of the time, Pallas kernels for 0%

commit v1 on v0

--- a/solution.py
+++ b/solution.py
@@ -6,6 +6,29 @@
 HEADS = 32
 HD = 128
 CLUSTERS = 128
+
+
+def cut_along(x, dim, size):
+    shape = x.shape
+    tiles = x.reshape(*shape[:dim], size, shape[dim] // size, *shape[dim + 1 :])
+    return jnp.moveaxis(tiles, dim, 0)
+
+
+def laid_out(parts, dim):
+    parts = jnp.moveaxis(parts, 0, dim)
+    dims = parts.shape
+    return parts.reshape(*dims[:dim], dims[dim] * dims[dim + 1], *dims[dim + 2 :])
+
+
+def exchange_in_pairs(x, axis, split_dim, concat_dim):
+    count, index = (lax.axis_size(axis), lax.axis_index(axis))
+    tiles = cut_along(x, split_dim, count)
+    outs = [tiles[index]]
+    for hop in range(1, count):
+        sent = tiles[index ^ hop]
+        outs.append(lax.ppermute(sent, axis, [(i, i ^ hop) for i in range(count)]))
+    tiles = jnp.stack(outs)[index ^ jnp.arange(count)]
+    return laid_out(tiles, concat_dim)
 
 
 def slot_table(block_ids, slot_depth):
@@ -60,7 +83,7 @@
     home_table = slot_table(group_ids, slot_depth)
     relaid = (
         lax.all_to_all(queries, "head", split_axis=1, concat_axis=0, tiled=True),
-        lax.all_to_all(keys, "head", split_axis=1, concat_axis=0, tiled=True),
+        exchange_in_pairs(keys, "head", 1, 0),
         lax.all_to_all(values, "head", split_axis=1, concat_axis=0, tiled=True),
     )
     stacked = jnp.stack([tensor.reshape(n_head, sub_rows, group_heads, HD) for tensor in relaid])

time: 418 us -> 406 us (0.971)
  waiting for transfers between devices: 232 us -> 220 us
  starting transfers between devices: 42.5 us -> 38.3 us
    all_to_all x1, waiting for transfers between devices: 11.9 us -> 2.16 us  [body(): lax.all_to_all(queries, 'head', split_axis=1, concat_axis=0, tiled=True)]
    all_to_all x1 -> x0, waiting for transfers between devices: 8.49 us -> none  [body(): lax.all_to_all(keys, 'head', split_axis=1, concat_axis=0, tiled=True)]
    all_to_all x1, starting transfers between devices: 19.1 us -> 14.6 us  [body(): lax.all_to_all(markers, 'seq', split_axis=2, concat_axis=2, tiled=True)]
  transfers between devices with their start and end apart: 7 -> 9, of which waited for: 5 -> 5; matrix products, arithmetic and copies ran while one was open for 15% -> 16% of each run, Pallas kernels for 0% -> 0%
where the time goes in v1:
time: 406 us; the launch traced here: 405 us
  waiting for transfers between devices  220 us (54%)
  blocking collectives  56.8 us (14%)
  starting transfers between devices  38.3 us (9%)
  local copies, waits for them, and re-layouts  36.1 us (9%)
  matrix products  28.3 us (7%)
  between operations  13.7 us (3%)
  other arithmetic  12.1 us (3%)
    all_to_all x1, waiting for transfers between devices, body(): lax.all_to_all(packed, 'seq', split_axis=2, concat_axis=2, tiled=True)  164 us
    all_to_all x1, blocking collectives, attend_and_return(): lax.all_to_all(result_block, 'seq', split_axis=1, concat_axis=1, tiled=True)  56.8 us
    reduce_scatter x1, waiting for transfers between devices, body(): lax.psum_scatter(partial_value.astype(jnp.bfloat16), 'head', scatter_dime...  44.1 us
    all_to_all x1, starting transfers between devices, body(): lax.all_to_all(markers, 'seq', split_axis=2, concat_axis=2, tiled=True)  14.6 us
    all_to_all x1, starting transfers between devices, body(): lax.all_to_all(packed, 'seq', split_axis=2, concat_axis=2, tiled=True)  10.5 us
    dot_general x1, matrix products, body(): jnp.dot(gathered, lax.all_gather(out_weight, 'seq', axis=1, tiled=True),...  9.5 us
    dot_general x1, matrix products, attend_blocks(): jnp.einsum('cqk,ckd->cqd', weights, packed[2], preferred_element_type=jnp...  9.4 us
  transfers between devices with their start and end apart: 9, of which 5 were waited for; matrix products, arithmetic and copies ran while one was open for 16% of the time, Pallas kernels for 0%

profile of v1, /device:TPU:1, one launch (start us, length us, event | category | flops | bytes accessed | tf_op | source)
XLA Modules:
  0.0 405.2 jit_solution(6133643032002982691)
XLA Ops:
  6.5 2.3 copy.82
  8.9 4.8 %all-to-all-start.1 = ((bf16[128,4,1024]{0,2,1:T(8,128)(2,1)}), bf16[128,4,1024]{0,2,1:T(8,128)(2,1)S(1)}, u32[]{:S(2)}, u32[]{:S(2)}) async-start(bf16[128,4,1024]{0,2,1:T(8,128)(2,1)} %bitcast.6), calls=%async_computation.1 | async-start | bytes 2097152 | tf_op jit(solution)/shard_map/all_to_all | solution.py:85
  15.3 1.5 collective-permute-start
  17.7 2.4 collective-permute-start.1
  20.0 0.9 copy.87
  21.9 2.3 copy.89
  24.8 2.2 all-to-all-done.1
  27.0 4.2 %all-to-all-start.2 = ((bf16[128,4,1024]{0,2,1:T(8,128)(2,1)}), bf16[128,4,1024]{0,2,1:T(8,128)(2,1)}, u32[]{:S(2)}, u32[]{:S(2)}) async-start(bf16[128,4,1024]{0,2,1:T(8,128)(2,1)} %bitcast.19), calls=%async_computation.2 | async-start | bytes 2097152 | tf_op jit(solution)/shard_map/all_to_all | solution.py:87
  31.2 2.5 multiply_reduce_fusion
  34.8 3.5 collective-permute-done.1
  38.3 1.2 pad_maximum_fusion
  40.2 1.3 copy.88
  41.5 1.6 copy.91
  43.1 1.3 copy.90
  44.5 5.1 %all-to-all-done.2 = bf16[128,4,1024]{0,2,1:T(8,128)(2,1)} async-done(((bf16[128,4,1024]{0,2,1:T(8,128)(2,1)}), bf16[128,4,1024]{0,2,1:T(8,128)(2,1)}, u32[]{:S(2)}, u32[]{:S(2)}) %all-to-all-start.2) | async-done | bytes 1048608 | tf_op jit(solution)/shard_map/all_to_all | solution.py:87
  49.5 14.6 %all-to-all-start = ((bf16[1,16,64,8]{1,3,0,2:T(8,128)(2,1)}), bf16[1,16,64,8]{1,3,0,2:T(8,128)(2,1)S(1)}, u32[]{:S(2)}, u32[]{:S(2)}) async-start(bf16[1,16,64,8]{1,3,0,2:T(8,128)(2,1)} %copy.80), calls=%async_computation | async-start | bytes 262144 | tf_op jit(solution)/shard_map/all_to_all | solution.py:101
  64.1 1.6 copy.92
  65.7 3.8 convert_bitcast_fusion
  69.5 2.6 copy.94
  72.2 6.7 %copy.95 = bf16[3,16,64,8,128]{4,1,3,0,2:T(8,128)(2,1)} copy(bf16[3,16,64,8,128]{4,2,1,3,0:T(8,128)(2,1)S(1)} %bitcast.73) | data formatting | bytes 12582912 | tf_op jit(solution)/shard_map/reshape | solution.py:93
  78.9 10.5 %all-to-all-start.3 = ((bf16[3,16,64,8,128]{4,1,3,0,2:T(8,128)(2,1)}), bf16[3,16,64,8,128]{4,1,3,0,2:T(8,128)(2,1)}, u32[]{:S(2)}, u32[]{:S(2)}) async-start(bf16[3,16,64,8,128]{4,1,3,0,2:T(8,128)(2,1)} %copy.95), calls=%async_computation.3 | async-start | bytes 12582912 | tf_op jit(solution)/shard_map/all_to_all | solution.py:100
  90.5 164.3 %all-to-all-done.3 = bf16[3,16,64,8,128]{4,1,3,0,2:T(8,128)(2,1)} async-done(((bf16[3,16,64,8,128]{4,1,3,0,2:T(8,128)(2,1)}), bf16[3,16,64,8,128]{4,1,3,0,2:T(8,128)(2,1)}, u32[]{:S(2)}, u32[]{:S(2)}) %all-to-all-start.3) | async-done | bytes 6291488 | tf_op jit(solution)/shard_map/all_to_all | solution.py:100
  254.8 6.0 %fusion.46 = (bf16[1,16,64,8,128]{4,1,3,0,2:T(8,128)(2,1)S(1)}, bf16[1,16,64,8,128]{4,1,3,0,2:T(8,128)(2,1)}, bf16[1,16,64,8,128]{4,1,3,0,2:T(8,128)(2,1)S(1)}) fusion(bf16[3,16,64,8,128]{4,1,3,0,2:T(8,128)(2,1)} %all-to-all-done.3), kind=kLoop, calls=%fused_computation.61 | loop fusion | bytes 12582912 | tf_op jit(solution)/shard_map/slice | solution.py:46
  260.8 2.4 fusion.14
  263.2 8.1 %fusion.47 = (f32[16,512]{1,0:T(8,128)S(1)}, f32[16,512,512]{1,2,0:T(8,128)}) fusion(f32[16,512,512]{1,2,0:T(8,128)S(1)} %fusion.14, pred[16,512]{1,0:T(8,128)(4,1)S(1)} %copy.81), kind=kOutput, calls=%fused_computation.62 | output fusion | flops 25166336 | bytes 33595392 | tf_op jit(solution)/shard_map/sub | solution.py:50
  271.3 9.4 %convert_bitcast_fusion.1 = bf16[16,64,8,128]{3,2,1,0:T(8,128)(2,1)S(1)} fusion(bf16[1,16,64,8,128]{4,1,3,0,2:T(8,128)(2,1)} %get-tuple-element.6, f32[16,512,512]{1,2,0:T(8,128)} %get-tuple-element.15, f32[16,512]{1,0:T(8,128)S(1)} %get-tuple-element.14), kind=kOutput, calls=%fused_computation.33 | convolution fusion | flops 1083179008 | bytes 21004288 | tf_op jit(solution)/shard_map/cqk,ckd->cqd/dot_general | solution.py:52
  280.7 2.4 copy.100
  283.2 56.8 %all_to_all.47 = bf16[16,64,8,128]{3,0,2,1:T(8,128)(2,1)S(1)} all-to-all(bf16[16,64,8,128]{3,0,2,1:T(8,128)(2,1)S(1)} %copy.100), channel_id=1, replica_groups=mesh['seq'=64,'head'=4] {'seq'}, dimensions={1} | all-to-all | bytes 4194304 | tf_op jit(solution)/shard_map/all_to_all | solution.py:67
  340.0 1.4 copy.101
  341.4 2.6 fusion.29
  344.7 9.5 %convolution_convert_fusion = bf16[512,4096]{1,0:T(8,128)(2,1)} fusion(bf16[1024,4096]{0,1:T(8,128)(2,1)} %all-gather.2.cloned.1.call-done, bf16[64,8,8,128]{3,2,1,0:T(8,128)(2,1)S(1)} %bitcast.78), kind=kOutput, calls=%fused_computation.11 | convolution fusion | flops 4297064448 | bytes 13631488 | tf_op jit(solution)/shard_map/dot_general | solution.py:109
  354.3 44.1 %reduce-scatter.2.cloned.1.call-done = bf16[512,1024]{1,0:T(8,128)(2,1)} async-done(((bf16[512,4096]{1,0:T(8,128)(2,1)}), bf16[512,1024]{1,0:T(8,128)(2,1)}) %reduce-scatter.2.cloned.1.call-update) | async-done | bytes 1048592 | tf_op jit(solution)/shard_map/reduce_scatter | solution.py:114
  (39 shorter events, 7.6 us)
Async XLA Ops:
  6.5 14.4 %copy-start = (s32[32,512,1]{1,2,0:T(1,128)S(1)}, s32[32,512,1]{1,2,0:T(1,128)}, u32[]{:S(2)}) copy-start(s32[32,512,1]{1,2,0:T(1,128)} %param.8) | copy-start | bytes 196612
  6.5 7.2 %copy-start.4 = (bf16[128,4096]{1,0:T(8,128)(2,1)S(1)}, bf16[128,4096]{1,0:T(8,128)(2,1)}, u32[]{:S(2)}) copy-start(bf16[128,4096]{1,0:T(8,128)(2,1)} %param.6) | copy-start | bytes 3145732
  8.9 18.1 %all-to-all-start.1 = ((bf16[128,4,1024]{0,2,1:T(8,128)(2,1)}), bf16[128,4,1024]{0,2,1:T(8,128)(2,1)S(1)}, u32[]{:S(2)}, u32[]{:S(2)}) async-start(bf16[128,4,1024]{0,2,1:T(8,128)(2,1)} %bitcast.6), calls=%async_computation.1 | async-start | bytes 2097152 | tf_op jit(solution)/shard_map/all_to_all | solution.py:85
  15.3 19.4 %collective-permute-start = (bf16[128,1024]{1,0:T(8,128)(2,1)}, bf16[128,1024]{1,0:T(8,128)(2,1)}, u32[]{:S(2)}, u32[]{:S(2)}) collective-permute-start(bf16[128,1024]{1,0:T(8,128)(2,1)} %bitcast.11), channel_id=1, source_target_pairs={{0,1},{1,0},{2,3},{3,2},{4,5},{5,4},{6,7},{7,6},{8,9},{9,8},{10,11... | collective-permute-start | bytes 786440 | tf_op jit(solution)/shard_map/ppermute | solution.py:29
  17.7 20.6 %collective-permute-start.1 = (bf16[128,1024]{1,0:T(8,128)(2,1)}, bf16[128,1024]{1,0:T(8,128)(2,1)}, u32[]{:S(2)}, u32[]{:S(2)}) collective-permute-start(bf16[128,1024]{1,0:T(8,128)(2,1)} %bitcast.13), channel_id=1, source_target_pairs={{0,2},{1,3},{2,0},{3,1},{4,6},{5,7},{6,4},{7,5},{8,10},{9,11},{10,... | collective-permute-start | bytes 786440 | tf_op jit(solution)/shard_map/ppermute | solution.py:29
  20.9 17.4 %collective-permute-start.2 = (bf16[128,1024]{1,0:T(8,128)(2,1)}, bf16[128,1024]{1,0:T(8,128)(2,1)}, u32[]{:S(2)}, u32[]{:S(2)}) collective-permute-start(bf16[128,1024]{1,0:T(8,128)(2,1)} %bitcast.15), channel_id=1, source_target_pairs={{0,3},{1,2},{2,1},{3,0},{4,7},{5,6},{6,5},{7,4},{8,11},{9,10},{10,... | collective-permute-start | bytes 786440 | tf_op jit(solution)/shard_map/ppermute | solution.py:29
  27.0 11.3 %copy-start.2 = (bf16[128,4,1024]{0,2,1:T(8,128)(2,1)}, bf16[128,4,1024]{0,2,1:T(8,128)(2,1)S(1)}, u32[]{:S(2)}) copy-start(bf16[128,4,1024]{0,2,1:T(8,128)(2,1)S(1)} %all-to-all-done.1) | copy-start | bytes 3145732
  27.0 22.6 %all-to-all-start.2 = ((bf16[128,4,1024]{0,2,1:T(8,128)(2,1)}), bf16[128,4,1024]{0,2,1:T(8,128)(2,1)}, u32[]{:S(2)}, u32[]{:S(2)}) async-start(bf16[128,4,1024]{0,2,1:T(8,128)(2,1)} %bitcast.19), calls=%async_computation.2 | async-start | bytes 2097152 | tf_op jit(solution)/shard_map/all_to_all | solution.py:87
  40.2 3.0 copy-start.3
  49.5 29.3 %all-to-all-start = ((bf16[1,16,64,8]{1,3,0,2:T(8,128)(2,1)}), bf16[1,16,64,8]{1,3,0,2:T(8,128)(2,1)S(1)}, u32[]{:S(2)}, u32[]{:S(2)}) async-start(bf16[1,16,64,8]{1,3,0,2:T(8,128)(2,1)} %copy.80), calls=%async_computation | async-start | bytes 262144 | tf_op jit(solution)/shard_map/all_to_all | solution.py:101
  78.9 175.9 %all-to-all-start.3 = ((bf16[3,16,64,8,128]{4,1,3,0,2:T(8,128)(2,1)}), bf16[3,16,64,8,128]{4,1,3,0,2:T(8,128)(2,1)}, u32[]{:S(2)}, u32[]{:S(2)}) async-start(bf16[3,16,64,8,128]{4,1,3,0,2:T(8,128)(2,1)} %copy.95), calls=%async_computation.3 | async-start | bytes 12582912 | tf_op jit(solution)/shard_map/all_to_all | solution.py:100
  89.4 255.3 %all-gather.2.cloned.1.call-start = ((), (), s32[]{:S(2)}) async-start(), calls=%async_computation.6 | async-start | bytes 8519680 | tf_op jit(solution)/shard_map/all_gather | solution.py:111
  90.1 308.3 %reduce-scatter.2.cloned.1.call-start = ((), (), s32[]{:S(2)}) async-start(), calls=%async_computation.7 | async-start | bytes 5242880 | tf_op jit(solution)/shard_map/reduce_scatter | solution.py:114
  344.7 53.7 %copy-start.1 = (s32[32,512,1]{1,2,0:T(1,128)S(1)}, s32[32,512,1]{1,2,0:T(1,128)}, u32[]{:S(2)}) copy-start(s32[32,512,1]{1,2,0:T(1,128)} %param.8) | copy-start | bytes 196612
Sparse Core Ops, SparseCore 0:
  93.0 134.2 all-gather.1
  354.4 43.9 reduce-scatter.1
